TPU v7x, 32 devices: a whole 2x2x4 slice. The times are simulated.
32 devices in a mesh: wave: 4 (over y, core), lev: 4 (over z), cpl: 2 (over x).
Axes of the slice: x: 2, y: 2, z: 4, core: 2. Of those that a mesh axis runs over, the one named last changes fastest.
Arguments:
- spectral: bfloat16 [1280, 2, 4, 24, 1280], P('wave', None, None, 'lev'), may hold values from -0.125 to 0.125
- legendre: bfloat16 [1280, 16, 1280], P('wave', 'cpl'), may hold values from -0.15625 to 0.15625
- wavenumber: int32 [1280], replicated, may hold values from 0 to 1279, each once
- level_weight: float32 [24], P('lev'), may hold values from 0.1 to 1
- source_row: int32 [16], replicated, may hold values from 0 to 14
- row_weight: float32 [16], replicated, may hold values from 0.2 to 0.8
Outputs:
- ocean_flux: float32 [16, 4, 4320], P(('wave', 'cpl'), None, 'lev')
All inputs are finite; a program needn't handle non-finite values.
Results may differ from a plain program's by a relative error of at most 0.0041.
Values may be sent and summed in bfloat16 or wider, within the bound.
No kernel may reach another device: no remote copies, remote signals or barrier semaphores. Data moves between devices by JAX's collectives and lax.ppermute only.
A program may use at most 192 MiB of HBM per device.

v0:
```python
import math
import jax
import jax.numpy as jnp
from jax import lax
from jax.sharding import PartitionSpec as P

NLON = 4320


def phase_angle(phase, lon_total):
    return phase.astype(jnp.float32) * (2.0 * math.pi / lon_total)


def surface_flux(grid_vals, level_weight):
    wind_speed = jnp.sqrt(grid_vals[..., 0, :, :] ** 2 + grid_vals[..., 1, :, :] ** 2 + 0.25)
    return jnp.sum(level_weight[:, None] * wind_speed[..., None, :, :] * grid_vals, axis=-2)


def latitude_order(gathered, wave_count, cpl_count, lat_dev):
    trailing = gathered.shape[1:]
    gathered = gathered.reshape((wave_count, cpl_count, lat_dev) + trailing)
    gathered = jnp.swapaxes(gathered, 0, 1)
    return gathered.reshape((wave_count * cpl_count * lat_dev,) + trailing)


def interpolate(gathered, source, weight_hi):
    lower = jnp.take(gathered, source, axis=0)
    upper = jnp.take(gathered, source + 1, axis=0)
    return (1.0 - weight_hi[:, None, None]) * lower + weight_hi[:, None, None] * upper


def local(spectral, legendre, wavenumber, level_weight, source_row, row_weight):
    slot_count = spectral.shape[0]
    fields = spectral.shape[2]
    levels = spectral.shape[3]
    degree = spectral.shape[4]
    channels = 2 * fields * levels
    wave_count = lax.axis_size("wave")
    cpl_count = lax.axis_size("cpl")
    wave_at = lax.axis_index("wave")
    cpl_at = lax.axis_index("cpl")
    owned_waves = lax.dynamic_slice_in_dim(wavenumber, wave_at * slot_count, slot_count)
    coefficient = spectral.reshape(slot_count, channels, degree)
    in_triangle = (
        lax.broadcasted_iota(jnp.int32, (slot_count, 1, degree), 2)
        < (degree - owned_waves)[:, None, None]
    )
    coefficient = jnp.where(in_triangle, coefficient, jnp.zeros_like(coefficient))
    spec_grid = jnp.einsum(
        "skj,slj->slk", coefficient, legendre, preferred_element_type=jnp.float32
    ).astype(jnp.bfloat16)
    by_latitude = lax.all_to_all(spec_grid, "wave", split_axis=1, concat_axis=0, tiled=True)
    total_slots = by_latitude.shape[0]
    lat_dev = by_latitude.shape[1]
    rows_in = (
        by_latitude.reshape(total_slots, lat_dev, 2, fields * levels)
        .transpose(1, 3, 0, 2)
        .reshape(lat_dev * fields * levels, 2 * total_slots)
    )
    lon_block = NLON // 8
    factor = jnp.where(wavenumber == 0, 1.0, 2.0).astype(jnp.float32)[:, None]
    offsets = jnp.arange(lon_block, dtype=jnp.int32)
    base_angle = phase_angle(wavenumber[:, None] * offsets[None, :] % NLON, NLON)
    base_cos = jnp.cos(base_angle)
    base_sin = jnp.sin(base_angle)

    def one_block(first_lon):
        start_angle = phase_angle(wavenumber * first_lon % NLON, NLON)[:, None]
        start_cos = jnp.cos(start_angle)
        start_sin = jnp.sin(start_angle)
        cos_vals = start_cos * base_cos - start_sin * base_sin
        sin_vals = start_sin * base_cos + start_cos * base_sin
        fourier = (
            jnp.stack([factor * cos_vals, -factor * sin_vals], axis=1)
            .astype(jnp.bfloat16)
            .reshape(2 * total_slots, lon_block)
        )
        grid_vals = jnp.dot(rows_in, fourier, preferred_element_type=jnp.float32).reshape(
            lat_dev, fields, levels, lon_block
        )
        return surface_flux(grid_vals, level_weight)

    block_starts = jnp.arange(8, dtype=jnp.int32) * lon_block
    per_block = lax.map(one_block, block_starts)
    partial_value = per_block.transpose(1, 2, 0, 3).reshape(lat_dev, fields, NLON)
    own_first = (wave_at * cpl_count + cpl_at) * lat_dev
    source = lax.dynamic_slice_in_dim(source_row, own_first, lat_dev)
    weight_hi = lax.dynamic_slice_in_dim(row_weight, own_first, lat_dev)
    strip_width = NLON // lax.axis_size("lev")
    summed = lax.psum(partial_value, "lev")
    gathered = lax.all_gather(summed, ("wave", "cpl"), axis=0, tiled=True)
    gathered = latitude_order(gathered, wave_count, cpl_count, lat_dev)
    gathered = lax.dynamic_slice_in_dim(
        gathered, lax.axis_index("lev") * strip_width, strip_width, 2
    )
    return interpolate(gathered, source, weight_hi)


def solution(mesh):
    placed = (P("wave", None, None, "lev", None), P("wave", "cpl", None), P(), P("lev"), P(), P())
    return jax.shard_map(
        local,
        mesh=mesh,
        in_specs=placed,
        out_specs=P(("wave", "cpl"), None, "lev"),
        check_vma=False,
    )
```

profile of v0, /device:TPU:0, one launch (start us, length us, event | category | flops | bytes accessed | tf_op | source)
XLA Modules:
  0.0 437.1 jit_solution(12876540771261802303)
XLA Ops:
  7.6 26.6 %copy.16 = bf16[320,2,4,6,1280]{4,0,3,2,1:T(8,128)(2,1)} copy(bf16[320,2,4,6,1280]{4,2,3,1,0:T(4,128)(2,1)} %param.10) | data formatting | bytes 78643200 | tf_op args[0]
  34.2 26.6 %bitcast_select_fusion = bf16[320,48,1280]{2,0,1:T(8,128)(2,1)} fusion(bf16[320,2,4,6,1280]{4,0,3,2,1:T(8,128)(2,1)} %copy.16, pred[320,1280]{1,0:T(8,128)(4,1)S(1)} %iota_compare_fusion), kind=kLoop, calls=%fused_computation.40 | loop fusion | flops 19660800 | bytes 79052800 | tf_op jit(solution)/shard_map/jit(_where)/select_n | solution.py:48
  60.8 47.0 %fusion.31 = bf16[320,8,48]{2,1,0:T(8,128)(2,1)S(1)} fusion(bf16[320,8,1280]{2,1,0:T(8,128)(2,1)} %param.11, bf16[320,48,1280]{2,0,1:T(8,128)(2,1)} %bitcast_select_fusion), kind=kOutput, calls=%fused_computation.45 | convolution fusion | flops 314695680 | bytes 46120960 | tf_op jit(solution)/shard_map/skj,slj->slk/dot_general | solution.py:49
  123.3 240.5 %while.14 = (s32[]{:T(128)}, f32[8,2,4,540]{3,2,1,0:T(4,128)}, f32[6]{0:T(128)S(1)}, f32[1280,1]{0,1:T(1,128)S(1)}, s32[8]{0:T(128)S(1)}, /*index=5*/s32[1280]{0...) while((s32[]{:T(128)}, f32[8,2,4,540]{3,2,1,0:T(4,128)}, ...), condition=%wide.region_2.3_spmd.clone.clone, body=%wide.region_0.2_spmd.clone.clone.sunk | while | flops 147317040 | bytes 22999700 | solution.py:84
  124.5 12.4 %fusion.47 = (bf16[1280,1,540]{0,2,1:T(8,128)(2,1)S(1)}, bf16[1280,1,540]{0,2,1:T(8,128)(2,1)S(1)}) fusion(s32[1280]{0:T(1024)S(1)} %get-tuple-element.302, f32[1280]{0:T(1024)S(1)} %get-tuple-element.273, f32[1280]{0:T(1024)S(1)} %get-tuple-element.274, f32[1280]{0:T(1024)S(1)} %reduce.4, f32[1280]{0:T(1024)S(1)} %reduce.5), kind=kLoop, calls=%fused_computation.12.clone.1 | loop fusion | flops 13132800 | bytes 2790400 | tf_op jit(solution)/shard_map/convert
  137.2 7.2 %copy.33 = bf16[1280,2,540]{2,1,0:T(2,128)(2,1)} copy(bf16[1280,2,540]{0,2,1:T(8,128)(2,1)S(1)} %pad_maximum_fusion.2) | data formatting | bytes 5529600 | tf_op jit(solution)/shard_map/while/body/eval_jaxpr/stack | solution.py:74
  144.4 6.6 %convert_element_type.80 = bf16[2560,540]{1,0:T(8,128)(2,1)S(1)} reshape(bf16[1280,2,540]{2,1,0:T(2,128)(2,1)} %copy.33) | data formatting | bytes 5529600 | tf_op jit(solution)/shard_map/while/body/eval_jaxpr/convert_element_type | solution.py:75
  154.6 12.4 %fusion.47 = (bf16[1280,1,540]{0,2,1:T(8,128)(2,1)S(1)}, bf16[1280,1,540]{0,2,1:T(8,128)(2,1)S(1)}) fusion(s32[1280]{0:T(1024)S(1)} %get-tuple-element.302, f32[1280]{0:T(1024)S(1)} %get-tuple-element.273, f32[1280]{0:T(1024)S(1)} %get-tuple-element.274, f32[1280]{0:T(1024)S(1)} %reduce.4, f32[1280]{0:T(1024)S(1)} %reduce.5), kind=kLoop, calls=%fused_computation.12.clone.1 | loop fusion | flops 13132800 | bytes 2790400 | tf_op jit(solution)/shard_map/convert
  167.3 7.2 %copy.33 = bf16[1280,2,540]{2,1,0:T(2,128)(2,1)} copy(bf16[1280,2,540]{0,2,1:T(8,128)(2,1)S(1)} %pad_maximum_fusion.2) | data formatting | bytes 5529600 | tf_op jit(solution)/shard_map/while/body/eval_jaxpr/stack | solution.py:74
  174.5 6.6 %convert_element_type.80 = bf16[2560,540]{1,0:T(8,128)(2,1)S(1)} reshape(bf16[1280,2,540]{2,1,0:T(2,128)(2,1)} %copy.33) | data formatting | bytes 5529600 | tf_op jit(solution)/shard_map/while/body/eval_jaxpr/convert_element_type | solution.py:75
  184.7 12.4 %fusion.47 = (bf16[1280,1,540]{0,2,1:T(8,128)(2,1)S(1)}, bf16[1280,1,540]{0,2,1:T(8,128)(2,1)S(1)}) fusion(s32[1280]{0:T(1024)S(1)} %get-tuple-element.302, f32[1280]{0:T(1024)S(1)} %get-tuple-element.273, f32[1280]{0:T(1024)S(1)} %get-tuple-element.274, f32[1280]{0:T(1024)S(1)} %reduce.4, f32[1280]{0:T(1024)S(1)} %reduce.5), kind=kLoop, calls=%fused_computation.12.clone.1 | loop fusion | flops 13132800 | bytes 2790400 | tf_op jit(solution)/shard_map/convert
  197.3 7.2 %copy.33 = bf16[1280,2,540]{2,1,0:T(2,128)(2,1)} copy(bf16[1280,2,540]{0,2,1:T(8,128)(2,1)S(1)} %pad_maximum_fusion.2) | data formatting | bytes 5529600 | tf_op jit(solution)/shard_map/while/body/eval_jaxpr/stack | solution.py:74
  214.7 12.4 %fusion.47 = (bf16[1280,1,540]{0,2,1:T(8,128)(2,1)S(1)}, bf16[1280,1,540]{0,2,1:T(8,128)(2,1)S(1)}) fusion(s32[1280]{0:T(1024)S(1)} %get-tuple-element.302, f32[1280]{0:T(1024)S(1)} %get-tuple-element.273, f32[1280]{0:T(1024)S(1)} %get-tuple-element.274, f32[1280]{0:T(1024)S(1)} %reduce.4, f32[1280]{0:T(1024)S(1)} %reduce.5), kind=kLoop, calls=%fused_computation.12.clone.1 | loop fusion | flops 13132800 | bytes 2790400 | tf_op jit(solution)/shard_map/convert
  227.4 7.2 %copy.33 = bf16[1280,2,540]{2,1,0:T(2,128)(2,1)} copy(bf16[1280,2,540]{0,2,1:T(8,128)(2,1)S(1)} %pad_maximum_fusion.2) | data formatting | bytes 5529600 | tf_op jit(solution)/shard_map/while/body/eval_jaxpr/stack | solution.py:74
  244.8 12.4 %fusion.47 = (bf16[1280,1,540]{0,2,1:T(8,128)(2,1)S(1)}, bf16[1280,1,540]{0,2,1:T(8,128)(2,1)S(1)}) fusion(s32[1280]{0:T(1024)S(1)} %get-tuple-element.302, f32[1280]{0:T(1024)S(1)} %get-tuple-element.273, f32[1280]{0:T(1024)S(1)} %get-tuple-element.274, f32[1280]{0:T(1024)S(1)} %reduce.4, f32[1280]{0:T(1024)S(1)} %reduce.5), kind=kLoop, calls=%fused_computation.12.clone.1 | loop fusion | flops 13132800 | bytes 2790400 | tf_op jit(solution)/shard_map/convert
  257.5 7.2 %copy.33 = bf16[1280,2,540]{2,1,0:T(2,128)(2,1)} copy(bf16[1280,2,540]{0,2,1:T(8,128)(2,1)S(1)} %pad_maximum_fusion.2) | data formatting | bytes 5529600 | tf_op jit(solution)/shard_map/while/body/eval_jaxpr/stack | solution.py:74
  274.9 12.4 %fusion.47 = (bf16[1280,1,540]{0,2,1:T(8,128)(2,1)S(1)}, bf16[1280,1,540]{0,2,1:T(8,128)(2,1)S(1)}) fusion(s32[1280]{0:T(1024)S(1)} %get-tuple-element.302, f32[1280]{0:T(1024)S(1)} %get-tuple-element.273, f32[1280]{0:T(1024)S(1)} %get-tuple-element.274, f32[1280]{0:T(1024)S(1)} %reduce.4, f32[1280]{0:T(1024)S(1)} %reduce.5), kind=kLoop, calls=%fused_computation.12.clone.1 | loop fusion | flops 13132800 | bytes 2790400 | tf_op jit(solution)/shard_map/convert
  287.5 7.2 %copy.33 = bf16[1280,2,540]{2,1,0:T(2,128)(2,1)} copy(bf16[1280,2,540]{0,2,1:T(8,128)(2,1)S(1)} %pad_maximum_fusion.2) | data formatting | bytes 5529600 | tf_op jit(solution)/shard_map/while/body/eval_jaxpr/stack | solution.py:74
  304.9 12.4 %fusion.47 = (bf16[1280,1,540]{0,2,1:T(8,128)(2,1)S(1)}, bf16[1280,1,540]{0,2,1:T(8,128)(2,1)S(1)}) fusion(s32[1280]{0:T(1024)S(1)} %get-tuple-element.302, f32[1280]{0:T(1024)S(1)} %get-tuple-element.273, f32[1280]{0:T(1024)S(1)} %get-tuple-element.274, f32[1280]{0:T(1024)S(1)} %reduce.4, f32[1280]{0:T(1024)S(1)} %reduce.5), kind=kLoop, calls=%fused_computation.12.clone.1 | loop fusion | flops 13132800 | bytes 2790400 | tf_op jit(solution)/shard_map/convert
  317.6 7.2 %copy.33 = bf16[1280,2,540]{2,1,0:T(2,128)(2,1)} copy(bf16[1280,2,540]{0,2,1:T(8,128)(2,1)S(1)} %pad_maximum_fusion.2) | data formatting | bytes 5529600 | tf_op jit(solution)/shard_map/while/body/eval_jaxpr/stack | solution.py:74
  335.0 12.4 %fusion.47 = (bf16[1280,1,540]{0,2,1:T(8,128)(2,1)S(1)}, bf16[1280,1,540]{0,2,1:T(8,128)(2,1)S(1)}) fusion(s32[1280]{0:T(1024)S(1)} %get-tuple-element.302, f32[1280]{0:T(1024)S(1)} %get-tuple-element.273, f32[1280]{0:T(1024)S(1)} %get-tuple-element.274, f32[1280]{0:T(1024)S(1)} %reduce.4, f32[1280]{0:T(1024)S(1)} %reduce.5), kind=kLoop, calls=%fused_computation.12.clone.1 | loop fusion | flops 13132800 | bytes 2790400 | tf_op jit(solution)/shard_map/convert
  347.7 7.2 %copy.33 = bf16[1280,2,540]{2,1,0:T(2,128)(2,1)} copy(bf16[1280,2,540]{0,2,1:T(8,128)(2,1)S(1)} %pad_maximum_fusion.2) | data formatting | bytes 5529600 | tf_op jit(solution)/shard_map/while/body/eval_jaxpr/stack | solution.py:74
  365.6 35.4 %all-reduce.2.cloned.1.call-done = f32[2,4,4320]{2,1,0:T(4,128)} async-done(((f32[2,4,4320]{2,1,0:T(4,128)}), f32[2,4,4320]{2,1,0:T(4,128)}) %all-reduce.2.cloned.1.call-update) | async-done | bytes 138256 | tf_op jit(solution)/shard_map/psum | solution.py:90
  401.2 25.6 %all-gather.2.cloned.1.call-done = f32[16,4,4320]{2,1,0:T(4,128)} async-done(((f32[2,4,4320]{2,1,0:T(4,128)}), f32[16,4,4320]{2,1,0:T(4,128)}) %all-gather.2.cloned.1.call-update) | async-done | bytes 1105936 | tf_op jit(solution)/shard_map/all_gather | solution.py:91
  (123 shorter events, 91.8 us)
Async XLA Ops:
  60.8 52.4 %copy-start = (s32[1280]{0:T(1024)S(1)}, s32[1280]{0:T(1024)}, u32[]{:S(2)}) copy-start(s32[1280]{0:T(1024)} %param.12) | copy-start | bytes 15364
  109.0 10.6 %all-to-all-start = ((bf16[320,8,48]{0,2,1:T(8,128)(2,1)}), bf16[320,8,48]{0,2,1:T(8,128)(2,1)S(1)}, u32[]{:S(2)}, u32[]{:S(2)}) async-start(bf16[320,8,48]{0,2,1:T(8,128)(2,1)} %copy.18), calls=%async_computation | async-start | bytes 589824 | tf_op jit(solution)/shard_map/all_to_all | solution.py:52
  113.2 287.8 %all-reduce.2.cloned.1.call-start = ((), (), s32[]{:S(2)}) async-start(), calls=%async_computation.1 | async-start | bytes 278528 | tf_op jit(solution)/shard_map/psum | solution.py:90
  113.2 10.0 %copy-start.1 = (f32[6]{0:T(128)S(1)}, f32[6]{0:T(128)}, u32[]{:S(2)}) copy-start(f32[6]{0:T(128)} %param.13) | copy-start | bytes 76
  123.3 277.8 %copy-start.2 = (f32[16]{0:T(128)S(1)}, f32[16]{0:T(128)}, u32[]{:S(2)}) copy-start(f32[16]{0:T(128)} %param.15) | copy-start | bytes 196
  123.3 277.9 %copy-start.3 = (s32[16]{0:T(128)S(1)}, s32[16]{0:T(128)}, u32[]{:S(2)}) copy-start(s32[16]{0:T(128)} %param.14) | copy-start | bytes 196
  365.6 61.3 %all-gather.2.cloned.1.call-start = ((), (), s32[]{:S(2)}) async-start(), calls=%async_computation.2 | async-start | bytes 1253376 | tf_op jit(solution)/shard_map/all_gather | solution.py:91
Sparse Core Ops, SparseCore 0:
  365.7 35.2 all-reduce.1
  403.0 23.7 all-gather.1
where the time goes:
time: 439 us; the launch traced here: 437 us
  local copies, waits for them, and re-layouts  156 us (36%)
  other arithmetic  136 us (31%)
  waiting for transfers between devices  67.4 us (15%)
  matrix products  59.3 us (14%)
  between operations  13.5 us (3%)
    another operation x24, other arithmetic  99.7 us
    another operation x8, local copies, waits for them, and re-layouts, one_block(): jnp.stack([factor * cos_vals, -factor * sin_vals], axis=1)  57.6 us
    convert_element_type x8, local copies, waits for them, and re-layouts, one_block(): fourier = jnp.stack([factor * cos_vals, -factor * sin_vals], axis=1).asty...  52.9 us
    dot_general x1, matrix products, local(): jnp.einsum('skj,slj->slk', coefficient, legendre, preferred_element_type=...  47 us
    psum x1, waiting for transfers between devices, local(): summed = lax.psum(partial_value, 'lev')  35.4 us
    unnamed x10, local copies, waits for them, and re-layouts  27.6 us
    select_n x1, other arithmetic, local(): jnp.where(in_triangle, coefficient, jnp.zeros_like(coefficient))  26.6 us
    all_gather x1, waiting for transfers between devices, local(): gathered = lax.all_gather(summed, ('wave', 'cpl'), axis=0, tiled=True)  25.6 us
  transfers between devices with their start and end apart: 3, of which 3 were waited for; matrix products, arithmetic and copies ran while one was open for 0% of the time, Pallas kernels for 0%

commit v1 on v0

--- a/solution.py
+++ b/solution.py
@@ -5,6 +5,12 @@
 from jax.sharding import PartitionSpec as P
 
 NLON = 4320
+
+
+def summed_here(array, name):
+    blocks = lax.all_gather(array, name, axis=0, tiled=False)
+    total = blocks.sum(axis=0)
+    return total
 
 
 def phase_angle(phase, lon_total):
@@ -87,7 +93,7 @@
     source = lax.dynamic_slice_in_dim(source_row, own_first, lat_dev)
     weight_hi = lax.dynamic_slice_in_dim(row_weight, own_first, lat_dev)
     strip_width = NLON // lax.axis_size("lev")
-    summed = lax.psum(partial_value, "lev")
+    summed = summed_here(partial_value, "lev")
     gathered = lax.all_gather(summed, ("wave", "cpl"), axis=0, tiled=True)
     gathered = latitude_order(gathered, wave_count, cpl_count, lat_dev)
     gathered = lax.dynamic_slice_in_dim(

time: 439 us -> 420 us (0.957)
  waiting for transfers between devices: 67.4 us -> 30.9 us
  blocking collectives: 0 us -> 16.6 us
    psum x1 -> x0, waiting for transfers between devices: 35.4 us -> none  [local(): summed = lax.psum(partial_value, 'lev')]
    all_gather x0 -> x1, blocking collectives: none -> 16.6 us  [summed_here(): blocks = lax.all_gather(array, name, axis=0, tiled=False)]
  transfers between devices with their start and end apart: 3 -> 2, of which waited for: 3 -> 2; matrix products, arithmetic and copies ran while one was open for 0% -> 0% of each run, Pallas kernels for 0% -> 0%
where the time goes in v1:
time: 420 us; the launch traced here: 419 us
  local copies, waits for them, and re-layouts  156 us (37%)
  other arithmetic  138 us (33%)
  matrix products  59.4 us (14%)
  waiting for transfers between devices  30.9 us (7%)
  blocking collectives  16.6 us (4%)
  between operations  13.5 us (3%)
  starting transfers between devices  4.24 us (1%)
    another operation x24, other arithmetic  99.7 us
    another operation x8, local copies, waits for them, and re-layouts, one_block(): jnp.stack([factor * cos_vals, -factor * sin_vals], axis=1)  58.2 us
    convert_element_type x8, local copies, waits for them, and re-layouts, one_block(): fourier = jnp.stack([factor * cos_vals, -factor * sin_vals], axis=1).asty...  52.9 us
    dot_general x1, matrix products, local(): jnp.einsum('skj,slj->slk', coefficient, legendre, preferred_element_type=...  47 us
    unnamed x10, local copies, waits for them, and re-layouts  27.6 us
    select_n x1, other arithmetic, local(): jnp.where(in_triangle, coefficient, jnp.zeros_like(coefficient))  26.6 us
    all_gather x1, waiting for transfers between devices, local(): gathered = lax.all_gather(summed, ('wave', 'cpl'), axis=0, tiled=True)  24.6 us
    all_gather x1, blocking collectives, summed_here(): blocks = lax.all_gather(array, name, axis=0, tiled=False)  16.6 us
  transfers between devices with their start and end apart: 2, of which 2 were waited for; matrix products, arithmetic and copies ran while one was open for 0% of the time, Pallas kernels for 0%

profile of v1, /device:TPU:0, one launch (start us, length us, event | category | flops | bytes accessed | tf_op | source)
XLA Modules:
  0.0 418.6 jit_solution(6933421772484680530)
XLA Ops:
  7.6 26.6 %copy.23 = bf16[320,2,4,6,1280]{4,0,3,2,1:T(8,128)(2,1)} copy(bf16[320,2,4,6,1280]{4,2,3,1,0:T(4,128)(2,1)} %param.10) | data formatting | bytes 78643200 | tf_op args[0]
  34.2 26.6 %bitcast_select_fusion = bf16[320,48,1280]{2,0,1:T(8,128)(2,1)} fusion(bf16[320,2,4,6,1280]{4,0,3,2,1:T(8,128)(2,1)} %copy.23, pred[320,1280]{1,0:T(8,128)(4,1)S(1)} %iota_compare_fusion), kind=kLoop, calls=%fused_computation.40 | loop fusion | flops 19660800 | bytes 79052800 | tf_op jit(solution)/shard_map/jit(_where)/select_n | solution.py:54
  60.9 47.0 %fusion.31 = bf16[320,8,48]{2,1,0:T(8,128)(2,1)S(1)} fusion(bf16[320,8,1280]{2,1,0:T(8,128)(2,1)} %param.11, bf16[320,48,1280]{2,0,1:T(8,128)(2,1)} %bitcast_select_fusion), kind=kOutput, calls=%fused_computation.45 | convolution fusion | flops 314695680 | bytes 46120960 | tf_op jit(solution)/shard_map/skj,slj->slk/dot_general | solution.py:55
  123.4 241.7 %while.14 = (s32[]{:T(128)}, f32[8,2,4,540]{3,2,1,0:T(4,128)}, f32[6]{0:T(128)S(1)}, f32[1280,1]{0,1:T(1,128)S(1)}, s32[8]{0:T(128)S(1)}, /*index=5*/s32[1280]{0...) while((s32[]{:T(128)}, f32[8,2,4,540]{3,2,1,0:T(4,128)}, ...), condition=%wide.region_2.3_spmd.clone.clone, body=%wide.region_0.2_spmd.clone.clone.sunk | while | flops 147317040 | bytes 22999700 | solution.py:90
  124.7 12.4 %fusion.47 = (bf16[1280,1,540]{0,2,1:T(8,128)(2,1)S(1)}, bf16[1280,1,540]{0,2,1:T(8,128)(2,1)S(1)}) fusion(s32[1280]{0:T(1024)S(1)} %get-tuple-element.310, f32[1280]{0:T(1024)S(1)} %get-tuple-element.281, f32[1280]{0:T(1024)S(1)} %get-tuple-element.282, f32[1280]{0:T(1024)S(1)} %reduce.4, f32[1280]{0:T(1024)S(1)} %reduce.5), kind=kLoop, calls=%fused_computation.12.clone.1 | loop fusion | flops 13132800 | bytes 2790400 | tf_op jit(solution)/shard_map/convert
  137.4 7.3 %copy.40 = bf16[1280,2,540]{2,1,0:T(2,128)(2,1)} copy(bf16[1280,2,540]{0,2,1:T(8,128)(2,1)S(1)} %pad_maximum_fusion.2) | data formatting | bytes 5529600 | tf_op jit(solution)/shard_map/while/body/eval_jaxpr/stack | solution.py:80
  144.7 6.6 %convert_element_type.80 = bf16[2560,540]{1,0:T(8,128)(2,1)S(1)} reshape(bf16[1280,2,540]{2,1,0:T(2,128)(2,1)} %copy.40) | data formatting | bytes 5529600 | tf_op jit(solution)/shard_map/while/body/eval_jaxpr/convert_element_type | solution.py:81
  154.9 12.4 %fusion.47 = (bf16[1280,1,540]{0,2,1:T(8,128)(2,1)S(1)}, bf16[1280,1,540]{0,2,1:T(8,128)(2,1)S(1)}) fusion(s32[1280]{0:T(1024)S(1)} %get-tuple-element.310, f32[1280]{0:T(1024)S(1)} %get-tuple-element.281, f32[1280]{0:T(1024)S(1)} %get-tuple-element.282, f32[1280]{0:T(1024)S(1)} %reduce.4, f32[1280]{0:T(1024)S(1)} %reduce.5), kind=kLoop, calls=%fused_computation.12.clone.1 | loop fusion | flops 13132800 | bytes 2790400 | tf_op jit(solution)/shard_map/convert
  167.6 7.3 %copy.40 = bf16[1280,2,540]{2,1,0:T(2,128)(2,1)} copy(bf16[1280,2,540]{0,2,1:T(8,128)(2,1)S(1)} %pad_maximum_fusion.2) | data formatting | bytes 5529600 | tf_op jit(solution)/shard_map/while/body/eval_jaxpr/stack | solution.py:80
  174.9 6.6 %convert_element_type.80 = bf16[2560,540]{1,0:T(8,128)(2,1)S(1)} reshape(bf16[1280,2,540]{2,1,0:T(2,128)(2,1)} %copy.40) | data formatting | bytes 5529600 | tf_op jit(solution)/shard_map/while/body/eval_jaxpr/convert_element_type | solution.py:81
  185.1 12.4 %fusion.47 = (bf16[1280,1,540]{0,2,1:T(8,128)(2,1)S(1)}, bf16[1280,1,540]{0,2,1:T(8,128)(2,1)S(1)}) fusion(s32[1280]{0:T(1024)S(1)} %get-tuple-element.310, f32[1280]{0:T(1024)S(1)} %get-tuple-element.281, f32[1280]{0:T(1024)S(1)} %get-tuple-element.282, f32[1280]{0:T(1024)S(1)} %reduce.4, f32[1280]{0:T(1024)S(1)} %reduce.5), kind=kLoop, calls=%fused_computation.12.clone.1 | loop fusion | flops 13132800 | bytes 2790400 | tf_op jit(solution)/shard_map/convert
  197.8 7.3 %copy.40 = bf16[1280,2,540]{2,1,0:T(2,128)(2,1)} copy(bf16[1280,2,540]{0,2,1:T(8,128)(2,1)S(1)} %pad_maximum_fusion.2) | data formatting | bytes 5529600 | tf_op jit(solution)/shard_map/while/body/eval_jaxpr/stack | solution.py:80
  215.3 12.4 %fusion.47 = (bf16[1280,1,540]{0,2,1:T(8,128)(2,1)S(1)}, bf16[1280,1,540]{0,2,1:T(8,128)(2,1)S(1)}) fusion(s32[1280]{0:T(1024)S(1)} %get-tuple-element.310, f32[1280]{0:T(1024)S(1)} %get-tuple-element.281, f32[1280]{0:T(1024)S(1)} %get-tuple-element.282, f32[1280]{0:T(1024)S(1)} %reduce.4, f32[1280]{0:T(1024)S(1)} %reduce.5), kind=kLoop, calls=%fused_computation.12.clone.1 | loop fusion | flops 13132800 | bytes 2790400 | tf_op jit(solution)/shard_map/convert
  228.0 7.3 %copy.40 = bf16[1280,2,540]{2,1,0:T(2,128)(2,1)} copy(bf16[1280,2,540]{0,2,1:T(8,128)(2,1)S(1)} %pad_maximum_fusion.2) | data formatting | bytes 5529600 | tf_op jit(solution)/shard_map/while/body/eval_jaxpr/stack | solution.py:80
  245.6 12.4 %fusion.47 = (bf16[1280,1,540]{0,2,1:T(8,128)(2,1)S(1)}, bf16[1280,1,540]{0,2,1:T(8,128)(2,1)S(1)}) fusion(s32[1280]{0:T(1024)S(1)} %get-tuple-element.310, f32[1280]{0:T(1024)S(1)} %get-tuple-element.281, f32[1280]{0:T(1024)S(1)} %get-tuple-element.282, f32[1280]{0:T(1024)S(1)} %reduce.4, f32[1280]{0:T(1024)S(1)} %reduce.5), kind=kLoop, calls=%fused_computation.12.clone.1 | loop fusion | flops 13132800 | bytes 2790400 | tf_op jit(solution)/shard_map/convert
  258.2 7.3 %copy.40 = bf16[1280,2,540]{2,1,0:T(2,128)(2,1)} copy(bf16[1280,2,540]{0,2,1:T(8,128)(2,1)S(1)} %pad_maximum_fusion.2) | data formatting | bytes 5529600 | tf_op jit(solution)/shard_map/while/body/eval_jaxpr/stack | solution.py:80
  275.8 12.4 %fusion.47 = (bf16[1280,1,540]{0,2,1:T(8,128)(2,1)S(1)}, bf16[1280,1,540]{0,2,1:T(8,128)(2,1)S(1)}) fusion(s32[1280]{0:T(1024)S(1)} %get-tuple-element.310, f32[1280]{0:T(1024)S(1)} %get-tuple-element.281, f32[1280]{0:T(1024)S(1)} %get-tuple-element.282, f32[1280]{0:T(1024)S(1)} %reduce.4, f32[1280]{0:T(1024)S(1)} %reduce.5), kind=kLoop, calls=%fused_computation.12.clone.1 | loop fusion | flops 13132800 | bytes 2790400 | tf_op jit(solution)/shard_map/convert
  288.4 7.3 %copy.40 = bf16[1280,2,540]{2,1,0:T(2,128)(2,1)} copy(bf16[1280,2,540]{0,2,1:T(8,128)(2,1)S(1)} %pad_maximum_fusion.2) | data formatting | bytes 5529600 | tf_op jit(solution)/shard_map/while/body/eval_jaxpr/stack | solution.py:80
  306.0 12.4 %fusion.47 = (bf16[1280,1,540]{0,2,1:T(8,128)(2,1)S(1)}, bf16[1280,1,540]{0,2,1:T(8,128)(2,1)S(1)}) fusion(s32[1280]{0:T(1024)S(1)} %get-tuple-element.310, f32[1280]{0:T(1024)S(1)} %get-tuple-element.281, f32[1280]{0:T(1024)S(1)} %get-tuple-element.282, f32[1280]{0:T(1024)S(1)} %reduce.4, f32[1280]{0:T(1024)S(1)} %reduce.5), kind=kLoop, calls=%fused_computation.12.clone.1 | loop fusion | flops 13132800 | bytes 2790400 | tf_op jit(solution)/shard_map/convert
  318.6 7.3 %copy.40 = bf16[1280,2,540]{2,1,0:T(2,128)(2,1)} copy(bf16[1280,2,540]{0,2,1:T(8,128)(2,1)S(1)} %pad_maximum_fusion.2) | data formatting | bytes 5529600 | tf_op jit(solution)/shard_map/while/body/eval_jaxpr/stack | solution.py:80
  336.2 12.4 %fusion.47 = (bf16[1280,1,540]{0,2,1:T(8,128)(2,1)S(1)}, bf16[1280,1,540]{0,2,1:T(8,128)(2,1)S(1)}) fusion(s32[1280]{0:T(1024)S(1)} %get-tuple-element.310, f32[1280]{0:T(1024)S(1)} %get-tuple-element.281, f32[1280]{0:T(1024)S(1)} %get-tuple-element.282, f32[1280]{0:T(1024)S(1)} %reduce.4, f32[1280]{0:T(1024)S(1)} %reduce.5), kind=kLoop, calls=%fused_computation.12.clone.1 | loop fusion | flops 13132800 | bytes 2790400 | tf_op jit(solution)/shard_map/convert
  348.9 7.3 %copy.40 = bf16[1280,2,540]{2,1,0:T(2,128)(2,1)} copy(bf16[1280,2,540]{0,2,1:T(8,128)(2,1)S(1)} %pad_maximum_fusion.2) | data formatting | bytes 5529600 | tf_op jit(solution)/shard_map/while/body/eval_jaxpr/stack | solution.py:80
  366.2 16.6 %all_gather.6 = f32[4,2,4,4320]{3,2,1,0:T(4,128)S(1)} all-gather(f32[1,2,4,4320]{3,2,1,0:T(4,128)S(1)} %all_gather_reshape.3), channel_id=1, replica_groups=mesh['wave'=4,'lev'=4,'cpl'=2] {'lev'}, dimensions={0}, use_global_device_ids=true | all-gather | bytes 691200 | tf_op jit(solution)/shard_map/all_gather | solution.py:11
  383.8 24.6 %all-gather.2.cloned.1.call-done = f32[16,4,4320]{2,1,0:T(4,128)} async-done(((f32[2,4,4320]{2,1,0:T(4,128)}), f32[16,4,4320]{2,1,0:T(4,128)}) %all-gather.2.cloned.1.call-update) | async-done | bytes 1105936 | tf_op jit(solution)/shard_map/all_gather | solution.py:97
  (122 shorter events, 92.5 us)
Async XLA Ops:
  60.9 52.4 %copy-start = (s32[1280]{0:T(1024)S(1)}, s32[1280]{0:T(1024)}, u32[]{:S(2)}) copy-start(s32[1280]{0:T(1024)} %param.12) | copy-start | bytes 15364
  109.0 10.6 %all-to-all-start = ((bf16[320,8,48]{0,2,1:T(8,128)(2,1)}), bf16[320,8,48]{0,2,1:T(8,128)(2,1)S(1)}, u32[]{:S(2)}, u32[]{:S(2)}) async-start(bf16[320,8,48]{0,2,1:T(8,128)(2,1)} %copy.25), calls=%async_computation | async-start | bytes 589824 | tf_op jit(solution)/shard_map/all_to_all | solution.py:58
  113.3 295.1 %all-gather.2.cloned.1.call-start = ((), (), s32[]{:S(2)}) async-start(), calls=%async_computation.1 | async-start | bytes 1253376 | tf_op jit(solution)/shard_map/all_gather | solution.py:97
  113.3 10.1 %copy-start.1 = (f32[6]{0:T(128)S(1)}, f32[6]{0:T(128)}, u32[]{:S(2)}) copy-start(f32[6]{0:T(128)} %param.13) | copy-start | bytes 76
  123.4 260.2 %copy-start.2 = (f32[16]{0:T(128)S(1)}, f32[16]{0:T(128)}, u32[]{:S(2)}) copy-start(f32[16]{0:T(128)} %param.15) | copy-start | bytes 196
  123.4 260.3 %copy-start.3 = (s32[16]{0:T(128)S(1)}, s32[16]{0:T(128)}, u32[]{:S(2)}) copy-start(s32[16]{0:T(128)} %param.14) | copy-start | bytes 196
Sparse Core Ops, SparseCore 0:
  383.7 24.5 all-gather.1
